TPU v7x, 256 devices: a whole 4x4x8 slice. The times are simulated.
256 devices in a mesh: az: 16 (over z_lo, x, core), tile: 16 (over y, z_hi).
Axes of the slice: x: 4, y: 4, z: 8 (z_hi: 4, z_lo: 2; z = z_hi * 2 + z_lo), core: 2. Of those that a mesh axis runs over, the one named last changes fastest.
Arguments:
- image: float32 [2, 8192, 2048], P(None, 'tile', 'az'), may hold values from -6 to 6
- tv_dual: float32 [2, 2, 8192, 2048], P(None, None, 'tile', 'az'), may hold values from -3 to 3
- data_dual: float32 [2, 1024, 64, 128], P(None, 'az', 'tile'), may hold values from -3 to 3
- echoes: bfloat16 [2, 1024, 64, 128], P(None, 'az', 'tile'), may hold values from -6 to 6
- row_steer: bfloat16 [2, 1024, 32, 256], P(None, None, 'tile'), may hold values from -0.375 to 0.375
- col_steer: float32 [2, 1024, 32, 16], P(None, None, 'tile'), may hold values from -1.5 to 1.5
- kernels: bfloat16 [8, 128, 128], replicated, may hold values from -0.5 to 0.5
- footprint: int32 [32, 16, 6], P(None, 'az'), may hold values from 0 to 63
- phase: int32 [32, 16, 6], P(None, 'az'), may hold values from 0 to 7
- aperture: int32 [1024], P('az'), may hold values from 0 to 1, as said below
Outputs:
- image_new: float32 [2, 8192, 2048], P(None, 'tile', 'az')
- tv_new: float32 [2, 2, 8192, 2048], P(None, None, 'tile', 'az')
- dual_new: float32 [2, 1024, 64, 128], P(None, 'az', 'tile')
Inputs may be any that keep to these rules, and one draw needn't show every extreme that they name: 0 inside up to three gaps of 64 consecutive pulses each (wrapping around the aperture), 1 elsewhere.
All inputs are finite; a program needn't handle non-finite values.
Results may differ from a plain program's by a relative error of at most 0.0025.
The roundings to bfloat16 on the way count: a program that leaves them out, or rounds other values in their place, can miss the bound.
Values may be sent and summed in bfloat16 or wider, within the bound.
No kernel may reach another device: no remote copies, remote signals or barrier semaphores. Data moves between devices by JAX's collectives and lax.ppermute only.
A program may use at most 64 MiB of HBM per device.

v0:
```python
import jax
import jax.numpy as jnp
from jax import lax
from jax.sharding import PartitionSpec as P

dual_step = 0.5
primal_step = 0.25
edge_limit = 1.5


def padded_2(block, sides, width):
    for axis, dim in sides:
        count = lax.axis_size(axis)
        forward = [(i, i + 1) for i in range(count - 1)]
        backward = [(target, source) for source, target in forward]
        low = lax.ppermute(
            lax.slice_in_dim(block, block.shape[dim] - width, None, axis=dim), axis, forward
        )
        high = lax.ppermute(lax.slice_in_dim(block, 0, width, axis=dim), axis, backward)
        block = jnp.concatenate([low, block, high], axis=dim)
    return block


def on_device(
    image, tv_dual, data_dual, echoes, row_steer, col_steer, kernels, footprint, phase, aperture
):
    highest = lax.Precision.HIGHEST
    az_index = lax.axis_index("az")
    tile_index = lax.axis_index("tile")
    az_count = lax.axis_size("az")
    tile_count = lax.axis_size("tile")
    strip_rows = image.shape[1]
    columns = image.shape[2]
    tiles_dev = row_steer.shape[2]
    tile_rows = row_steer.shape[3]
    rows_dev = data_dual.shape[2]
    range_rows = rows_dev * tile_count
    foot_block = footprint[:, 0, :]
    phase_block = phase[:, 0, :]
    foot_mine = lax.dynamic_slice_in_dim(foot_block, tile_index * tiles_dev, tiles_dev, 0)
    phase_mine = lax.dynamic_slice_in_dim(phase_block, tile_index * tiles_dev, tiles_dev, 0)
    steer_re = row_steer[0]
    steer_im = row_steer[1]
    col_mine = lax.dynamic_slice_in_dim(col_steer, az_index, 1, 3)[..., 0]
    image_b = image.astype(jnp.bfloat16).reshape(2, tiles_dev, tile_rows, columns)
    part_sre = steer_re
    part_sim = steer_im
    weight_re = col_mine[0][..., None]
    weight_im = col_mine[1][..., None]
    prod_re = jnp.einsum("pjh,jhu->pju", part_sre, image_b[0], preferred_element_type=jnp.float32)
    prod_re = prod_re - jnp.einsum(
        "pjh,jhu->pju", part_sim, image_b[1], preferred_element_type=jnp.float32
    )
    prod_im = jnp.einsum("pjh,jhu->pju", part_sre, image_b[1], preferred_element_type=jnp.float32)
    prod_im = prod_im + jnp.einsum(
        "pjh,jhu->pju", part_sim, image_b[0], preferred_element_type=jnp.float32
    )
    real_part = weight_re * prod_re - weight_im * prod_im
    imag_part = weight_re * prod_im + weight_im * prod_re
    summed = lax.psum_scatter(
        jnp.stack([real_part, imag_part], axis=0), "az", scatter_dimension=1, tiled=True
    )
    projection_b = jnp.transpose(summed, (2, 1, 0, 3)).astype(jnp.bfloat16)
    all_proj = lax.all_gather(projection_b, "tile", axis=0, tiled=True)
    phase_ids = jnp.arange(kernels.shape[0], dtype=jnp.int32)
    my_rows = tile_index * rows_dev + jnp.arange(rows_dev, dtype=jnp.int32)
    hits = (foot_block[:, :, None, None] == my_rows[None, None, :, None]) & (
        phase_block[:, :, None, None] == phase_ids[None, None, None, :]
    )
    counts = jnp.sum(hits.astype(jnp.int32), axis=1).astype(jnp.bfloat16)
    grouped = jnp.einsum("jkq,jpcu->kqpcu", counts, all_proj, preferred_element_type=jnp.float32)
    forward = jnp.einsum("kqpcu,quv->cpkv", grouped, kernels.astype(jnp.float32), precision=highest)
    kern_mine = kernels[phase_mine]
    live = (aperture == 1)[None, :, None, None]
    dual_new = jnp.where(
        live,
        (data_dual + dual_step * (forward - echoes.astype(jnp.float32))) / (1.0 + dual_step),
        0.0,
    )
    dual_b = dual_new.astype(jnp.bfloat16)
    all_rows = lax.all_gather(dual_b, "tile", axis=2, tiled=True)
    chosen = jnp.take(all_rows, foot_mine, axis=2)
    back = jnp.einsum("cpjfv,jfuv->cjpu", chosen, kern_mine, preferred_element_type=jnp.float32)
    back_b = back.astype(jnp.bfloat16)
    piece = lax.all_gather(back_b, "az", axis=2, tiled=True)
    weight_re = col_mine[0].T[..., None]
    weight_im = col_mine[1].T[..., None]
    back_re = piece[0].astype(jnp.float32)
    back_im = piece[1].astype(jnp.float32)
    mixed_re = (weight_re * back_re + weight_im * back_im).astype(jnp.bfloat16)
    mixed_im = (weight_re * back_im - weight_im * back_re).astype(jnp.bfloat16)
    part_sre = steer_re
    part_sim = steer_im
    grad_re = jnp.einsum("pjh,jpu->jhu", part_sre, mixed_re, preferred_element_type=jnp.float32)
    grad_re = grad_re + jnp.einsum(
        "pjh,jpu->jhu", part_sim, mixed_im, preferred_element_type=jnp.float32
    )
    grad_im = jnp.einsum("pjh,jpu->jhu", part_sre, mixed_im, preferred_element_type=jnp.float32)
    grad_im = grad_im - jnp.einsum(
        "pjh,jpu->jhu", part_sim, mixed_re, preferred_element_type=jnp.float32
    )
    adjoint = jnp.stack([grad_re, grad_im])
    adjoint = adjoint.reshape(2, strip_rows, columns)
    stacked = jnp.concatenate([image, tv_dual.reshape(4, strip_rows, columns)], axis=0)
    padded = padded_2(stacked, (("az", 2), ("tile", 1)), 1)
    image_pad = padded[:2]
    dual_pad = padded[2:].reshape(2, 2, strip_rows + 2, columns + 2)
    total_rows = tile_count * strip_rows
    total_cols = az_count * columns
    global_row = tile_index * strip_rows - 1 + jnp.arange(strip_rows + 1, dtype=jnp.int32)
    global_col = az_index * columns - 1 + jnp.arange(columns + 1, dtype=jnp.int32)
    centre = image_pad[:, : strip_rows + 1, : columns + 1]
    grad_rows = image_pad[:, 1 : strip_rows + 2, : columns + 1] - centre
    grad_rows = jnp.where((global_row < total_rows - 1)[None, :, None], grad_rows, 0.0)
    grad_cols = image_pad[:, : strip_rows + 1, 1 : columns + 2] - centre
    grad_cols = jnp.where((global_col < total_cols - 1)[None, None, :], grad_cols, 0.0)
    moved = dual_pad[:, :, : strip_rows + 1, : columns + 1] + dual_step * jnp.stack(
        [grad_rows, grad_cols]
    )
    magnitude = jnp.sqrt(jnp.sum(moved * moved, axis=(0, 1)))
    projected = moved / jnp.maximum(1.0, magnitude / edge_limit)
    inside = (global_row >= 0)[:, None] & (global_col >= 0)[None, :]
    projected = jnp.where(inside[None, None], projected, 0.0)
    rows_part = jnp.where((global_row < total_rows - 1)[None, :, None], projected[0], 0.0)
    cols_part = jnp.where((global_col < total_cols - 1)[None, None, :], projected[1], 0.0)
    divergence = (
        rows_part[:, 1:, 1:] - rows_part[:, :-1, 1:] + cols_part[:, 1:, 1:] - cols_part[:, 1:, :-1]
    )
    image_new = image - primal_step * (adjoint - divergence)
    tv_new = projected[:, :, 1:, 1:]
    return (image_new, tv_new, dual_new)


def solution(mesh):
    in_specs = (
        P(None, "tile", "az"),
        P(None, None, "tile", "az"),
        P(None, "az", "tile", None),
        P(None, "az", "tile", None),
        P(None, None, "tile", None),
        P(None, None, "tile", None),
        P(),
        P(None, "az", None),
        P(None, "az", None),
        P("az"),
    )
    out_specs = (P(None, "tile", "az"), P(None, None, "tile", "az"), P(None, "az", "tile", None))
    return jax.shard_map(
        on_device, mesh=mesh, in_specs=in_specs, out_specs=out_specs, check_vma=False
    )
```

profile of v0, /device:TPU:1, one launch (start us, length us, event | category | flops | bytes accessed | tf_op | source)
XLA Modules:
  0.0 264.6 jit_solution(16992743149203517460)
XLA Ops:
  7.3 2.7 %fusion.64 = (bf16[1,1024,2,256]{3,2,1,0:T(2,128)(2,1)S(1)}, bf16[1,1024,2,256]{3,2,1,0:T(2,128)(2,1)S(1)}) fusion(bf16[2,1024,2,256]{3,2,1,0:T(2,128)(2,1)} %param.14), kind=kLoop, calls=%fused_computation.122 | loop fusion | bytes 4194304 | tf_op jit(solution)/shard_map/slice | solution.py:43
  11.0 1.5 fusion.44
  15.4 2.3 copy.117
  17.8 66.7 %all-reduce.2 = bf16[2,1024,2,128]{3,2,0,1:T(2,128)(2,1)S(1)} all-reduce(f32[2,1024,2,128]{3,2,0,1:T(2,128)} %copy.117), channel_id=2, replica_groups=mesh['az'=16,'tile'=16] {'az'}, use_global_device_ids=true, to_apply=%region_1.0.clone | all-reduce | flops 524288 | bytes 3145728
  86.7 56.0 %all-gather.4.cloned.1.call-done = bf16[32,64,2,128]{3,1,2,0:T(8,128)(2,1)} async-done(((bf16[2,64,2,128]{3,1,2,0:T(8,128)(2,1)}), bf16[32,64,2,128]{3,1,2,0:T(8,128)(2,1)}) %all-gather.4.cloned.1.call-update) | async-done | bytes 1048592 | tf_op jit(solution)/shard_map/all_gather | solution.py:64
  142.7 2.0 fusion.38
  144.8 2.3 fusion.66
  147.2 1.6 slice_maximum_fusion
  148.8 1.9 copy.132
  150.7 5.0 %collective-permute-start = (f32[6,512,1]{1,2,0:T(1,128)S(1)}, f32[6,512,1]{1,2,0:T(1,128)S(1)}, u32[]{:S(2)}, u32[]{:S(2)}) collective-permute-start(f32[6,512,1]{1,2,0:T(1,128)S(1)} %copy.132), channel_id=1, source_target_pairs={{0,16},{16,32},{32,48},{48,64},{64,80},{80,96},{96,112},{112,128},... | collective-permute-start | bytes 36872 | tf_op jit(solution)/shard_map/ppermute | solution.py:16
  156.1 1.9 collective-permute-start.1
  162.5 2.0 collective-permute-start.2
  164.5 1.5 collective-permute-start.3
  166.0 38.9 %all-gather.6.cloned.1.call-done = bf16[2,64,64,128]{3,1,0,2:T(8,128)(2,1)} async-done(((bf16[2,64,4,128]{3,1,0,2:T(8,128)(2,1)}), bf16[2,64,64,128]{3,1,0,2:T(8,128)(2,1)}) %all-gather.6.cloned.1.call-update) | async-done | bytes 2097168 | tf_op jit(solution)/shard_map/all_gather | solution.py:81
  204.9 2.9 %gather_fusion.1 = bf16[12,2,64,128]{3,2,1,0:T(8,128)(2,1)} fusion(bf16[2,64,64,128]{3,1,0,2:T(8,128)(2,1)} %all-gather.6.cloned.1.call-done, s32[1024]{0:T(1024)S(1)} %pad_clamp_fusion), kind=kCustom, calls=%fused_computation.1 | custom fusion | bytes 786480 | tf_op jit(solution)/shard_map/jit(_take)/gather | solution.py:82
  207.8 2.1 fusion.25
  210.1 2.2 pad_maximum_fusion
  218.3 25.4 %all-gather.8.cloned.1.call-done = bf16[2,2,1024,128]{3,2,0,1:T(8,128)(2,1)} async-done(((bf16[2,2,64,128]{3,2,0,1:T(8,128)(2,1)}), bf16[2,2,1024,128]{3,2,0,1:T(8,128)(2,1)}) %all-gather.8.cloned.1.call-update) | async-done | bytes 1048592 | tf_op jit(solution)/shard_map/all_gather | solution.py:85
  243.7 2.4 fusion.42
  246.2 2.0 fusion.7
  248.1 1.8 copy.128
  249.9 2.4 fusion.41
  252.3 2.0 fusion.8
  255.4 2.7 %fusion.47 = f32[2,512,128]{2,1,0:T(8,128)} fusion(f32[2,512,128]{2,1,0:T(8,128)S(1)} %copy-done.5, f32[2,513,129]{2,1,0:T(8,128)} %get-tuple-element.21, f32[2,513,129]{2,1,0:T(8,128)S(1)} %get-tuple-element.20, f32[1,512,128]{2,1,0:T(8,128)S(1)} %bitcast.164, f32[1,512,128]{2,1,0:T(8,128)S(1)} %bitcast.163), kind=kLoop, calls=%fused_computation.75 | loop fusion | flops 917504 | bytes 3670016 | tf_op jit(solution)/shard_map/sub | solution.py:129
  (97 shorter events, 17.5 us)
Async XLA Ops:
  7.2 137.6 %copy-start = (bf16[8,128,128]{2,1,0:T(8,128)(2,1)S(1)}, bf16[8,128,128]{2,1,0:T(8,128)(2,1)}, u32[]{:S(2)}) copy-start(bf16[8,128,128]{2,1,0:T(8,128)(2,1)} %param.16) | copy-start | bytes 786436
  7.2 135.5 %all-gather.4.cloned.1.call-start = ((), (), s32[]{:S(2)}) async-start(), calls=%async_computation | async-start | bytes 1114112 | tf_op jit(solution)/shard_map/all_gather | solution.py:64
  7.2 2.8 %copy-start.3 = (f32[2,512,128]{2,1,0:T(8,128)S(1)}, f32[2,512,128]{2,1,0:T(8,128)}, u32[]{:S(2)}) copy-start(f32[2,512,128]{2,1,0:T(8,128)} %param.10) | copy-start | bytes 1572868
  10.0 3.8 %copy-start.6 = (bf16[1,1024,2,256]{3,2,1,0:T(2,128)(2,1)}, bf16[1,1024,2,256]{3,2,1,0:T(2,128)(2,1)S(1)}, u32[]{:S(2)}) copy-start(bf16[1,1024,2,256]{3,2,1,0:T(2,128)(2,1)S(1)} %get-tuple-element.24) | copy-start | bytes 3145732
  17.7 66.8 %copy-start.20 = (u32[256]{0:T(256)S(1)}, u32[256]{0:T(256)}, u32[]{:S(2)}) copy-start(u32[256]{0:T(256)} %constant.75) | copy-start | bytes 3076
  17.7 68.8 %copy-start.15 = (s32[32,1,6]{0,1,2:T(1,128)S(1)}, s32[32,1,6]{0,1,2:T(1,128)}, u32[]{:S(2)}) copy-start(s32[32,1,6]{0,1,2:T(1,128)} %param.17) | copy-start | bytes 2308
  17.7 68.8 %copy-start.16 = (s32[32,1,6]{0,1,2:T(1,128)S(1)}, s32[32,1,6]{0,1,2:T(1,128)}, u32[]{:S(2)}) copy-start(s32[32,1,6]{0,1,2:T(1,128)} %param.18) | copy-start | bytes 2308
  17.7 69.0 %copy-start.19 = (s32[64]{0:T(128)S(1)}, s32[64]{0:T(128)}, u32[]{:S(2)}) copy-start(s32[64]{0:T(128)} %param.19) | copy-start | bytes 772
  86.5 118.4 %all-gather.6.cloned.1.call-start = ((), (), s32[]{:S(2)}) async-start(), calls=%async_computation.1 | async-start | bytes 2228224 | tf_op jit(solution)/shard_map/all_gather | solution.py:81
  86.7 58.0 %copy-start.13 = (f32[2,64,4,128]{3,2,1,0:T(4,128)S(1)}, f32[2,64,4,128]{3,2,1,0:T(4,128)}, u32[]{:S(2)}) copy-start(f32[2,64,4,128]{3,2,1,0:T(4,128)} %param.12) | copy-start | bytes 786436
  86.7 58.0 %copy-start.14 = (bf16[2,64,4,128]{3,2,1,0:T(4,128)(2,1)S(1)}, bf16[2,64,4,128]{3,2,1,0:T(4,128)(2,1)}, u32[]{:S(2)}) copy-start(bf16[2,64,4,128]{3,2,1,0:T(4,128)(2,1)} %param.13) | copy-start | bytes 393220
  144.8 2.4 copy-start.1
  147.1 96.6 %all-gather.8.cloned.1.call-start = ((), (), s32[]{:S(2)}) async-start(), calls=%async_computation.2 | async-start | bytes 1114112 | tf_op jit(solution)/shard_map/all_gather | solution.py:85
  150.7 9.3 %collective-permute-start = (f32[6,512,1]{1,2,0:T(1,128)S(1)}, f32[6,512,1]{1,2,0:T(1,128)S(1)}, u32[]{:S(2)}, u32[]{:S(2)}) collective-permute-start(f32[6,512,1]{1,2,0:T(1,128)S(1)} %copy.132), channel_id=1, source_target_pairs={{0,16},{16,32},{32,48},{48,64},{64,80},{80,96},{96,112},{112,128},... | collective-permute-start | bytes 36872 | tf_op jit(solution)/shard_map/ppermute | solution.py:16
  156.1 5.0 %collective-permute-start.1 = (f32[6,512,1]{1,2,0:T(1,128)S(1)}, f32[6,512,1]{1,2,0:T(1,128)S(1)}, u32[]{:S(2)}, u32[]{:S(2)}) collective-permute-start(f32[6,512,1]{1,2,0:T(1,128)S(1)} %copy.133), channel_id=1, source_target_pairs={{16,0},{32,16},{48,32},{64,48},{80,64},{96,80},{112,96},{128,112},... | collective-permute-start | bytes 36872 | tf_op jit(solution)/shard_map/ppermute | solution.py:19
  162.5 47.5 %collective-permute-start.2 = (f32[6,1,130]{2,1,0:T(1,128)S(1)}, f32[6,1,130]{2,1,0:T(1,128)S(1)}, u32[]{:S(2)}, u32[]{:S(2)}) collective-permute-start(f32[6,1,130]{2,1,0:T(1,128)S(1)} %get-tuple-element.19), channel_id=1, source_target_pairs={{0,1},{1,2},{2,3},{3,4},{4,5},{5,6},{6,7},{7,8},{8,9},{9,10},{10,1... | collective-permute-start | bytes 9368 | tf_op jit(solution)/shard_map/ppermute | solution.py:16
  164.5 45.6 %collective-permute-start.3 = (f32[6,1,130]{2,1,0:T(1,128)S(1)}, f32[6,1,130]{2,1,0:T(1,128)S(1)}, u32[]{:S(2)}, u32[]{:S(2)}) collective-permute-start(f32[6,1,130]{2,1,0:T(1,128)S(1)} %get-tuple-element.18), channel_id=1, source_target_pairs={{1,0},{2,1},{3,2},{4,3},{5,4},{6,5},{7,6},{8,7},{9,8},{10,9},{11,1... | collective-permute-start | bytes 9368 | tf_op jit(solution)/shard_map/ppermute | solution.py:19
  210.0 2.3 copy-start.2
  216.2 27.5 %copy-start.9 = (bf16[1,1024,2,256]{3,2,1,0:T(2,128)(2,1)S(1)}, bf16[1,1024,2,256]{3,2,1,0:T(2,128)(2,1)}, u32[]{:S(2)}) copy-start(bf16[1,1024,2,256]{3,2,1,0:T(2,128)(2,1)} %copy-done.8) | copy-start | bytes 3145732
  243.7 2.5 copy-start.7
  243.7 2.5 copy-start.17
  249.9 2.4 copy-start.18
  252.3 3.1 %copy-start.5 = (f32[2,512,128]{2,1,0:T(8,128)S(1)}, f32[2,512,128]{2,1,0:T(8,128)}, u32[]{:S(2)}) copy-start(f32[2,512,128]{2,1,0:T(8,128)} %param.10) | copy-start | bytes 1572868
  252.3 3.1 %copy-start.11 = (f32[2,256,128]{2,1,0:T(8,128)S(1)}, f32[2,256,128]{2,1,0:T(8,128)}, u32[]{:S(2)}) copy-start(f32[2,256,128]{2,1,0:T(8,128)} %copy.128) | copy-start | bytes 786436
  (4 other events, 5.7 us)
Sparse Core Ops, SparseCore 0:
  86.6 56.0 all-gather.3
  147.2 57.5 all-gather.5
  210.0 33.6 all-gather.7
where the time goes:
time: 265 us
  waiting for transfers between devices  121 us (46%)
  blocking collectives  66.7 us (25%)
  local copies, waits for them, and re-layouts  21.7 us (8%)
  matrix products  18.1 us (7%)
  between operations  15 us (6%)
  other arithmetic  11.7 us (4%)
  starting transfers between devices  10.4 us (4%)
    unnamed x1, blocking collectives  66.7 us
    all_gather x1, waiting for transfers between devices, on_device(): all_proj = lax.all_gather(projection_b, 'tile', axis=0, tiled=True)  56 us
    all_gather x1, waiting for transfers between devices, on_device(): all_rows = lax.all_gather(dual_b, 'tile', axis=2, tiled=True)  38.9 us
    all_gather x1, waiting for transfers between devices, on_device(): piece = lax.all_gather(back_b, 'az', axis=2, tiled=True)  25.4 us
    ppermute x2, starting transfers between devices, padded_2(): lax.ppermute(lax.slice_in_dim(block, block.shape[dim] - width, None, axis...  6.92 us
  transfers between devices with their start and end apart: 7, of which 4 were waited for; matrix products, arithmetic and copies ran while one was open for 8% of the time, Pallas kernels for 0%

commit v1 on v0

--- a/solution.py
+++ b/solution.py
@@ -6,6 +6,12 @@
 dual_step = 0.5
 primal_step = 0.25
 edge_limit = 1.5
+bring_skins = lambda arr_in, named_axis: jnp.concatenate(
+    lax.all_to_all(
+        jnp.stack(lax.psum(1, axis_name=named_axis) * [arr_in], axis=0), named_axis, 0, 0
+    ),
+    axis=0,
+)
 
 
 def padded_2(block, sides, width):
@@ -61,7 +67,7 @@
         jnp.stack([real_part, imag_part], axis=0), "az", scatter_dimension=1, tiled=True
     )
     projection_b = jnp.transpose(summed, (2, 1, 0, 3)).astype(jnp.bfloat16)
-    all_proj = lax.all_gather(projection_b, "tile", axis=0, tiled=True)
+    all_proj = bring_skins(projection_b, "tile")
     phase_ids = jnp.arange(kernels.shape[0], dtype=jnp.int32)
     my_rows = tile_index * rows_dev + jnp.arange(rows_dev, dtype=jnp.int32)
     hits = (foot_block[:, :, None, None] == my_rows[None, None, :, None]) & (

time: 265 us -> 249 us (0.940)
  waiting for transfers between devices: 121 us -> 92.2 us
  starting transfers between devices: 10.4 us -> 21.1 us
  local copies, waits for them, and re-layouts: 21.7 us -> 24.5 us
    all_gather x1 -> x0, waiting for transfers between devices: 56 us -> none  [on_device(): all_proj = lax.all_gather(projection_b, 'tile', axis=0, tiled=True)]
    all_to_all x0 -> x1, waiting for transfers between devices: none -> 25.3 us  [lax.all_to_all(jnp.stack(lax.psum(1, axis_name=named_axis) * [arr_in], ax...]
    all_to_all x0 -> x1, starting transfers between devices: none -> 10 us  [lax.all_to_all(jnp.stack(lax.psum(1, axis_name=named_axis) * [arr_in], ax...]
    ppermute x2, starting transfers between devices: 3.39 us -> 6.07 us  [padded_2(): lax.ppermute(lax.slice_in_dim(block, 0, width, axis=dim), axis, backward)]
  transfers between devices with their start and end apart: 7 -> 7, of which waited for: 4 -> 3; matrix products, arithmetic and copies ran while one was open for 8% -> 9% of each run, Pallas kernels for 0% -> 0%
where the time goes in v1:
time: 249 us; the launch traced here: 248 us
  waiting for transfers between devices  92.2 us (37%)
  blocking collectives  66.7 us (27%)
  local copies, waits for them, and re-layouts  24.5 us (10%)
  starting transfers between devices  21.1 us (8%)
  matrix products  16.5 us (7%)
  between operations  15.3 us (6%)
  other arithmetic  11.7 us (5%)
    unnamed x1, blocking collectives  66.7 us
    all_gather x1, waiting for transfers between devices, on_device(): all_rows = lax.all_gather(dual_b, 'tile', axis=2, tiled=True)  41.5 us
    all_gather x1, waiting for transfers between devices, on_device(): piece = lax.all_gather(back_b, 'az', axis=2, tiled=True)  25.4 us
    all_to_all x1, waiting for transfers between devices, lax.all_to_all(jnp.stack(lax.psum(1, axis_name=named_axis) * [arr_in], ax...  25.3 us
    all_to_all x1, starting transfers between devices, lax.all_to_all(jnp.stack(lax.psum(1, axis_name=named_axis) * [arr_in], ax...  10 us
    ppermute x2, starting transfers between devices, padded_2(): lax.ppermute(lax.slice_in_dim(block, 0, width, axis=dim), axis, backward)  6.07 us
  transfers between devices with their start and end apart: 7, of which 3 were waited for; matrix products, arithmetic and copies ran while one was open for 9% of the time, Pallas kernels for 0%

profile of v1, /device:TPU:1, one launch (start us, length us, event | category | flops | bytes accessed | tf_op | source)
XLA Modules:
  0.0 248.0 jit_solution(8014998258224987105)
XLA Ops:
  7.2 2.7 %fusion.62 = (bf16[1,1024,2,256]{3,2,1,0:T(2,128)(2,1)S(1)}, bf16[1,1024,2,256]{3,2,1,0:T(2,128)(2,1)S(1)}) fusion(bf16[2,1024,2,256]{3,2,1,0:T(2,128)(2,1)} %param.14), kind=kLoop, calls=%fused_computation.120 | loop fusion | bytes 4194304 | tf_op jit(solution)/shard_map/slice | solution.py:49
  15.4 2.3 copy.118
  17.7 66.7 %all-reduce.2 = bf16[2,1024,2,128]{3,2,0,1:T(2,128)(2,1)S(1)} all-reduce(f32[2,1024,2,128]{3,2,0,1:T(2,128)} %copy.118), channel_id=2, replica_groups=mesh['az'=16,'tile'=16] {'az'}, use_global_device_ids=true, to_apply=%region_1.0.clone | all-reduce | flops 524288 | bytes 3145728
  85.8 1.8 stack.23
  87.6 10.0 %all-to-all-start = ((bf16[16,2,64,2,128]{4,1,3,2,0:T(2,128)(2,1)}), bf16[16,2,64,2,128]{4,1,3,2,0:T(2,128)(2,1)S(1)}, u32[]{:S(2)}, u32[]{:S(2)}) async-start(bf16[16,2,64,2,128]{4,1,3,2,0:T(2,128)(2,1)} %stack.23), calls=%async_computation | async-start | bytes 2097152 | tf_op jit(solution)/shard_map/all_to_all | solution.py:10
  97.9 25.3 %all-to-all-done = bf16[16,2,64,2,128]{4,1,3,2,0:T(2,128)(2,1)S(1)} async-done(((bf16[16,2,64,2,128]{4,1,3,2,0:T(2,128)(2,1)}), bf16[16,2,64,2,128]{4,1,3,2,0:T(2,128)(2,1)S(1)}, u32[]{:S(2)}, u32[]{:S(2)}) %all-to-all-start) | async-done | bytes 1048608 | tf_op jit(solution)/shard_map/all_to_all | solution.py:10
  125.3 2.3 fusion.64
  127.7 1.6 slice_maximum_fusion
  129.3 1.9 copy.132
  131.2 2.8 %collective-permute-start = (f32[6,512,1]{1,2,0:T(1,128)S(1)}, f32[6,512,1]{1,2,0:T(1,128)S(1)}, u32[]{:S(2)}, u32[]{:S(2)}) collective-permute-start(f32[6,512,1]{1,2,0:T(1,128)S(1)} %copy.132), channel_id=1, source_target_pairs={{0,16},{16,32},{32,48},{48,64},{64,80},{80,96},{96,112},{112,128},... | collective-permute-start | bytes 36872 | tf_op jit(solution)/shard_map/ppermute | solution.py:22
  134.5 4.6 %collective-permute-start.1 = (f32[6,512,1]{1,2,0:T(1,128)S(1)}, f32[6,512,1]{1,2,0:T(1,128)S(1)}, u32[]{:S(2)}, u32[]{:S(2)}) collective-permute-start(f32[6,512,1]{1,2,0:T(1,128)S(1)} %copy.133), channel_id=1, source_target_pairs={{16,0},{32,16},{48,32},{64,48},{80,64},{96,80},{112,96},{128,112},... | collective-permute-start | bytes 36872 | tf_op jit(solution)/shard_map/ppermute | solution.py:25
  142.9 2.0 collective-permute-start.2
  145.0 1.5 collective-permute-start.3
  146.5 41.5 %all-gather.3.cloned.1.call-done = bf16[2,64,64,128]{3,1,0,2:T(8,128)(2,1)} async-done(((bf16[2,64,4,128]{3,1,0,2:T(8,128)(2,1)}), bf16[2,64,64,128]{3,1,0,2:T(8,128)(2,1)}) %all-gather.3.cloned.1.call-update) | async-done | bytes 2097168 | tf_op jit(solution)/shard_map/all_gather | solution.py:87
  188.0 2.9 %gather_fusion.1 = bf16[12,2,64,128]{3,2,1,0:T(8,128)(2,1)} fusion(bf16[2,64,64,128]{3,1,0,2:T(8,128)(2,1)} %all-gather.3.cloned.1.call-done, s32[1024]{0:T(1024)S(1)} %pad_clamp_fusion), kind=kCustom, calls=%fused_computation.1 | custom fusion | bytes 786480 | tf_op jit(solution)/shard_map/jit(_take)/gather | solution.py:88
  190.9 2.1 fusion.25
  193.2 2.2 pad_maximum_fusion
  201.4 25.4 %all-gather.5.cloned.1.call-done = bf16[2,2,1024,128]{3,2,0,1:T(8,128)(2,1)} async-done(((bf16[2,2,64,128]{3,2,0,1:T(8,128)(2,1)}), bf16[2,2,1024,128]{3,2,0,1:T(8,128)(2,1)}) %all-gather.5.cloned.1.call-update) | async-done | bytes 1048592 | tf_op jit(solution)/shard_map/all_gather | solution.py:91
  226.8 2.4 fusion.39
  229.3 2.0 fusion.7
  231.2 1.8 copy.128
  233.0 2.4 fusion.38
  235.5 2.0 fusion.8
  238.5 2.7 %fusion.44 = f32[2,512,128]{2,1,0:T(8,128)} fusion(f32[2,512,128]{2,1,0:T(8,128)S(1)} %copy-done.5, f32[2,513,129]{2,1,0:T(8,128)} %get-tuple-element.21, f32[2,513,129]{2,1,0:T(8,128)S(1)} %get-tuple-element.20, f32[1,512,128]{2,1,0:T(8,128)S(1)} %bitcast.166, f32[1,512,128]{2,1,0:T(8,128)S(1)} %bitcast.165), kind=kLoop, calls=%fused_computation.72 | loop fusion | flops 917504 | bytes 3670016 | tf_op jit(solution)/shard_map/sub | solution.py:135
  (97 shorter events, 19.7 us)
Async XLA Ops:
  7.2 117.5 %copy-start = (bf16[8,128,128]{2,1,0:T(8,128)(2,1)S(1)}, bf16[8,128,128]{2,1,0:T(8,128)(2,1)}, u32[]{:S(2)}) copy-start(bf16[8,128,128]{2,1,0:T(8,128)(2,1)} %param.16) | copy-start | bytes 786436
  7.2 2.8 %copy-start.3 = (f32[2,512,128]{2,1,0:T(8,128)S(1)}, f32[2,512,128]{2,1,0:T(8,128)}, u32[]{:S(2)}) copy-start(f32[2,512,128]{2,1,0:T(8,128)} %param.10) | copy-start | bytes 1572868
  10.0 3.9 %copy-start.6 = (bf16[1,1024,2,256]{3,2,1,0:T(2,128)(2,1)}, bf16[1,1024,2,256]{3,2,1,0:T(2,128)(2,1)S(1)}, u32[]{:S(2)}) copy-start(bf16[1,1024,2,256]{3,2,1,0:T(2,128)(2,1)S(1)} %get-tuple-element.24) | copy-start | bytes 3145732
  13.3 1.2 copy-start.10
  17.7 66.7 %copy-start.20 = (u32[256]{0:T(256)S(1)}, u32[256]{0:T(256)}, u32[]{:S(2)}) copy-start(u32[256]{0:T(256)} %constant.75) | copy-start | bytes 3076
  85.8 11.9 %copy-start.15 = (s32[32,1,6]{0,1,2:T(1,128)S(1)}, s32[32,1,6]{0,1,2:T(1,128)}, u32[]{:S(2)}) copy-start(s32[32,1,6]{0,1,2:T(1,128)} %param.17) | copy-start | bytes 2308
  85.8 11.9 %copy-start.16 = (s32[32,1,6]{0,1,2:T(1,128)S(1)}, s32[32,1,6]{0,1,2:T(1,128)}, u32[]{:S(2)}) copy-start(s32[32,1,6]{0,1,2:T(1,128)} %param.18) | copy-start | bytes 2308
  85.8 12.0 %copy-start.19 = (s32[64]{0:T(128)S(1)}, s32[64]{0:T(128)}, u32[]{:S(2)}) copy-start(s32[64]{0:T(128)} %param.19) | copy-start | bytes 772
  87.6 35.5 %all-to-all-start = ((bf16[16,2,64,2,128]{4,1,3,2,0:T(2,128)(2,1)}), bf16[16,2,64,2,128]{4,1,3,2,0:T(2,128)(2,1)S(1)}, u32[]{:S(2)}, u32[]{:S(2)}) async-start(bf16[16,2,64,2,128]{4,1,3,2,0:T(2,128)(2,1)} %stack.23), calls=%async_computation | async-start | bytes 2097152 | tf_op jit(solution)/shard_map/all_to_all | solution.py:10
  97.6 90.4 %all-gather.3.cloned.1.call-start = ((), (), s32[]{:S(2)}) async-start(), calls=%async_computation.1 | async-start | bytes 2228224 | tf_op jit(solution)/shard_map/all_gather | solution.py:87
  125.3 2.4 copy-start.1
  127.6 99.2 %all-gather.5.cloned.1.call-start = ((), (), s32[]{:S(2)}) async-start(), calls=%async_computation.2 | async-start | bytes 1114112 | tf_op jit(solution)/shard_map/all_gather | solution.py:91
  131.2 9.9 %collective-permute-start = (f32[6,512,1]{1,2,0:T(1,128)S(1)}, f32[6,512,1]{1,2,0:T(1,128)S(1)}, u32[]{:S(2)}, u32[]{:S(2)}) collective-permute-start(f32[6,512,1]{1,2,0:T(1,128)S(1)} %copy.132), channel_id=1, source_target_pairs={{0,16},{16,32},{32,48},{48,64},{64,80},{80,96},{96,112},{112,128},... | collective-permute-start | bytes 36872 | tf_op jit(solution)/shard_map/ppermute | solution.py:22
  134.5 7.1 %collective-permute-start.1 = (f32[6,512,1]{1,2,0:T(1,128)S(1)}, f32[6,512,1]{1,2,0:T(1,128)S(1)}, u32[]{:S(2)}, u32[]{:S(2)}) collective-permute-start(f32[6,512,1]{1,2,0:T(1,128)S(1)} %copy.133), channel_id=1, source_target_pairs={{16,0},{32,16},{48,32},{64,48},{80,64},{96,80},{112,96},{128,112},... | collective-permute-start | bytes 36872 | tf_op jit(solution)/shard_map/ppermute | solution.py:25
  142.9 50.2 %collective-permute-start.2 = (f32[6,1,130]{2,1,0:T(1,128)S(1)}, f32[6,1,130]{2,1,0:T(1,128)S(1)}, u32[]{:S(2)}, u32[]{:S(2)}) collective-permute-start(f32[6,1,130]{2,1,0:T(1,128)S(1)} %get-tuple-element.19), channel_id=1, source_target_pairs={{0,1},{1,2},{2,3},{3,4},{4,5},{5,6},{6,7},{7,8},{8,9},{9,10},{10,1... | collective-permute-start | bytes 9368 | tf_op jit(solution)/shard_map/ppermute | solution.py:22
  145.0 48.2 %collective-permute-start.3 = (f32[6,1,130]{2,1,0:T(1,128)S(1)}, f32[6,1,130]{2,1,0:T(1,128)S(1)}, u32[]{:S(2)}, u32[]{:S(2)}) collective-permute-start(f32[6,1,130]{2,1,0:T(1,128)S(1)} %get-tuple-element.18), channel_id=1, source_target_pairs={{1,0},{2,1},{3,2},{4,3},{5,4},{6,5},{7,6},{8,7},{9,8},{10,9},{11,1... | collective-permute-start | bytes 9368 | tf_op jit(solution)/shard_map/ppermute | solution.py:25
  193.2 2.3 copy-start.2
  193.2 2.3 copy-start.4
  199.3 27.5 %copy-start.9 = (bf16[1,1024,2,256]{3,2,1,0:T(2,128)(2,1)S(1)}, bf16[1,1024,2,256]{3,2,1,0:T(2,128)(2,1)}, u32[]{:S(2)}) copy-start(bf16[1,1024,2,256]{3,2,1,0:T(2,128)(2,1)} %copy-done.8) | copy-start | bytes 3145732
  226.8 2.5 copy-start.7
  226.8 2.5 copy-start.17
  233.0 2.4 copy-start.18
  235.4 3.1 %copy-start.5 = (f32[2,512,128]{2,1,0:T(8,128)S(1)}, f32[2,512,128]{2,1,0:T(8,128)}, u32[]{:S(2)}) copy-start(f32[2,512,128]{2,1,0:T(8,128)} %param.10) | copy-start | bytes 1572868
  235.4 3.1 %copy-start.11 = (f32[2,256,128]{2,1,0:T(8,128)S(1)}, f32[2,256,128]{2,1,0:T(8,128)}, u32[]{:S(2)}) copy-start(f32[2,256,128]{2,1,0:T(8,128)} %copy.128) | copy-start | bytes 786436
  (4 other events, 4.1 us)
Sparse Core Ops, SparseCore 0:
  127.7 60.2 all-gather.2
  193.1 33.6 all-gather.4
